TPU v7x, 256 devices: a whole 4x4x8 slice. The times are simulated.
256 devices in a mesh: cfg: 2 (over core), req: 8 (over z), seq: 16 (over y, x).
Axes of the slice: x: 4, y: 4, z: 8, core: 2. Of those that a mesh axis runs over, the one named last changes fastest.
Arguments:
- img_hidden: bfloat16 [2, 16, 512, 1536], P('cfg', 'req', 'seq'), may hold values from -6 to 6
- txt_hidden: bfloat16 [2, 16, 160, 1536], P('cfg', 'req', 'seq'), may hold values from -6 to 6
- text_len: int32 [2, 16], P('cfg'), may hold values from 1 to 154, as said below
- pooled: float32 [2, 16, 1536], P('cfg'), may hold values from -6 to 6
- timestep: int32 [16], replicated, may hold values from 0 to 27
- latent: float32 [16, 512, 64], P('req', 'seq', 'cfg'), may hold values from -24 to 24
- mod_weight: bfloat16 [1536, 15360], P(None, ('req', 'seq')), may hold values from -0.15625 to 0.15625
- mod_bias: float32 [15360], P(('req', 'seq')), may hold values from -2 to 2
- img_qkv: bfloat16 [1536, 3, 1536], P(None, None, 'req'), may hold values from -2.5 to 2.5
- txt_kv: bfloat16 [1536, 2, 1536], P(None, None, 'req'), may hold values from -0.15625 to 0.15625
- out_weight: bfloat16 [1536, 1536], P('req'), may hold values from -0.15625 to 0.15625
- fc_in: bfloat16 [1536, 6144], P(None, 'seq'), may hold values from -0.15625 to 0.15625
- fc_out: bfloat16 [6144, 1536], P('seq'), may hold values from -0.078125 to 0.078125
- final_weight: bfloat16 [1536, 64], replicated, may hold values from -0.15625 to 0.15625
Outputs:
- velocity: float32 [16, 512, 64], P('req', 'seq', 'cfg')
- next_latent: float32 [16, 512, 64], P('req', 'seq', 'cfg')
- latent_norm: float32 [16], P('req')
- latent_peak: float32 [16], P('req')
Inputs may be any that keep to these rules, and one draw needn't show every extreme that they name: Text slots from text_len to 159 of a request are padding; every draw has a request of length 154 and one of length 1.
All inputs are finite; a program needn't handle non-finite values.
Results may differ from a plain program's by a relative error of at most 0.015.
Values may be sent and summed in bfloat16 or wider, within the bound.
No kernel may reach another device: no remote copies, remote signals or barrier semaphores. Data moves between devices by JAX's collectives and lax.ppermute only.
A program may use at most 64 MiB of HBM per device.

v0:
```python
import math
import jax
import jax.numpy as jnp
from jax import lax
from jax.sharding import PartitionSpec as P

D = 1536
HD = 64
PATCHC = 64
IMG = 512
STEPS = 28
SIGMA_SHIFT = 3.0
GUIDANCE = 5.0
EPSILON = 1e-06
MASKED_SCORE = -1e30


def from_partner(value, axis, distance):
    mask = 2**distance
    pairs = [(source, source ^ mask) for source in range(lax.axis_size(axis))]
    return lax.ppermute(value, axis, pairs)


def shifted(fraction):
    return SIGMA_SHIFT * fraction / (1.0 + (SIGMA_SHIFT - 1.0) * fraction)


def plan(timestep):
    position = timestep.astype(jnp.float32)
    return (shifted(1.0 - position / STEPS), shifted(1.0 - (position + 1.0) / STEPS))


def time_features(sigma):
    half_width = D // 2
    frequency = jnp.exp(-math.log(10000.0) * jnp.arange(half_width, dtype=jnp.float32) / half_width)
    angles = (1000.0 * sigma)[:, None] * frequency[None, :]
    return jnp.concatenate([jnp.cos(angles), jnp.sin(angles)], axis=1)


def layer_norm(values):
    average = jnp.mean(values, axis=-1, keepdims=True)
    centred = values - average
    spread = jnp.mean(centred * centred, axis=-1, keepdims=True)
    return centred * lax.rsqrt(spread + EPSILON)


def attention(queries, key_rows, value_rows, live_keys):
    query_count = queries.shape[0]
    head_count = queries.shape[1]
    block_rows = min(512, query_count)
    scale_factor = HD ** (-0.5)

    def one_block(query_block):
        scores = (
            jnp.einsum("qhd,khd->hqk", query_block, key_rows, preferred_element_type=jnp.float32)
            * scale_factor
        )
        scores = jnp.where(live_keys[None, None, :], scores, MASKED_SCORE)
        highest = jnp.max(scores, axis=-1, keepdims=True)
        exp_scores = jnp.exp(scores - highest)
        weights = (exp_scores / jnp.sum(exp_scores, axis=-1, keepdims=True)).astype(jnp.bfloat16)
        mixture = jnp.einsum(
            "hqk,khd->qhd", weights, value_rows, preferred_element_type=jnp.float32
        )
        return mixture.astype(jnp.bfloat16)

    blocks = queries.reshape(query_count // block_rows, block_rows, head_count, HD)
    return lax.map(one_block, blocks).reshape(query_count, head_count * HD)


def on_device(
    img_hidden,
    txt_hidden,
    text_len,
    pooled,
    timestep,
    latent,
    mod_weight,
    mod_bias,
    img_qkv,
    txt_kv,
    out_weight,
    fc_in,
    fc_out,
    final_weight,
):
    group_size = img_hidden.shape[1]
    current, upcoming = plan(timestep)
    activated = jax.nn.silu(pooled[0] + time_features(current)).astype(jnp.bfloat16)
    columns = jnp.dot(activated, mod_weight, preferred_element_type=jnp.float32) + mod_bias
    every_mod = lax.all_gather(columns, ("req", "seq"), axis=1, tiled=True)
    offset = lax.axis_index("req") * group_size
    modulation = lax.dynamic_slice_in_dim(every_mod, offset, group_size, 0).reshape(
        group_size, 10, 1, D
    )
    shift_attn, scale_attn, gate_attn = (modulation[:, 0], modulation[:, 1], modulation[:, 2])
    shift_mlp, scale_mlp, gate_mlp = (modulation[:, 3], modulation[:, 4], modulation[:, 5])
    shift_text, scale_text = (modulation[:, 6], modulation[:, 7])
    scale_final, shift_final = (modulation[:, 8], modulation[:, 9])
    img_float = img_hidden[0].astype(jnp.float32)
    img_in = (layer_norm(img_float) * (1.0 + scale_attn) + shift_attn).astype(jnp.bfloat16)
    txt_in = (
        layer_norm(txt_hidden[0].astype(jnp.float32)) * (1.0 + scale_text) + shift_text
    ).astype(jnp.bfloat16)
    all_img, all_txt = (
        lax.all_gather(img_in, "req", axis=0, tiled=True),
        lax.all_gather(txt_in, "req", axis=0, tiled=True),
    )
    head_width = img_qkv.shape[2]
    local_heads = head_width // HD
    qkv_columns = img_qkv.reshape(D, 3 * head_width)
    kv_columns = txt_kv.reshape(D, 2 * head_width)
    own_img, own_txt = (
        lax.all_to_all(all_img, "seq", split_axis=0, concat_axis=1, tiled=True),
        lax.all_to_all(all_txt, "seq", split_axis=0, concat_axis=1, tiled=True),
    )
    own_proj = jnp.einsum(
        "rnd,dc->rnc", own_img, qkv_columns, preferred_element_type=jnp.float32
    ).astype(jnp.bfloat16)
    own_proj_txt = jnp.einsum(
        "rnd,dc->rnc", own_txt, kv_columns, preferred_element_type=jnp.float32
    ).astype(jnp.bfloat16)
    local_count = own_proj.shape[0]
    image_rows = own_proj.shape[1]
    text_rows = own_proj_txt.shape[1]
    first_request = lax.axis_index("seq") * local_count

    def attend_request(operands):
        projected, projected_txt, request_slot = operands
        queries = projected[:, :head_width]
        key_rows = jnp.concatenate(
            [projected[:, head_width : 2 * head_width], projected_txt[:, :head_width]], axis=0
        )
        value_rows = jnp.concatenate(
            [projected[:, 2 * head_width :], projected_txt[:, head_width:]], axis=0
        )
        text_count = lax.dynamic_index_in_dim(text_len[0], first_request + request_slot, 0, False)
        live_keys = jnp.arange(image_rows + text_rows, dtype=jnp.int32) < image_rows + text_count
        total_keys = image_rows + text_rows
        return attention(
            queries.reshape(image_rows, local_heads, HD),
            key_rows.reshape(total_keys, local_heads, HD),
            value_rows.reshape(total_keys, local_heads, HD),
            live_keys,
        )

    attended = lax.map(
        attend_request, (own_proj, own_proj_txt, jnp.arange(local_count, dtype=jnp.int32))
    )
    projected_rows = jnp.einsum(
        "rnk,kd->rnd", attended, out_weight, preferred_element_type=jnp.float32
    )
    moved_rows = lax.all_to_all(
        projected_rows.astype(jnp.bfloat16), "seq", split_axis=1, concat_axis=0, tiled=True
    ).astype(projected_rows.dtype)
    attn_out = lax.psum_scatter(
        moved_rows.astype(jnp.bfloat16), "req", scatter_dimension=0, tiled=True
    ).astype(jnp.float32)
    img_mid = img_float + gate_attn * attn_out
    mlp_in = (layer_norm(img_mid) * (1.0 + scale_mlp) + shift_mlp).astype(jnp.bfloat16)
    raised = jnp.einsum(
        "rnd,df->rnf",
        lax.all_gather(mlp_in, "seq", axis=1, tiled=True),
        fc_in,
        preferred_element_type=jnp.float32,
    )
    hidden = jax.nn.gelu(raised, approximate=True).astype(jnp.bfloat16)
    mlp_terms = jnp.einsum("rnf,fd->rnd", hidden, fc_out, preferred_element_type=jnp.float32)
    mlp_out = lax.psum_scatter(
        mlp_terms.astype(jnp.bfloat16), "seq", scatter_dimension=1, tiled=True
    ).astype(jnp.float32)
    img_out = img_mid + gate_mlp * mlp_out
    final_in = (layer_norm(img_out) * (1.0 + scale_final) + shift_final).astype(jnp.bfloat16)
    own_velocity = jnp.einsum(
        "rnd,dc->rnc", final_in, final_weight, preferred_element_type=jnp.float32
    )
    half_values = latent.shape[2]
    half_index = lax.axis_index("cfg")
    kept_velocity = lax.dynamic_slice_in_dim(own_velocity, half_index * half_values, half_values, 2)
    sent_velocity = lax.dynamic_slice_in_dim(
        own_velocity, (1 - half_index) * half_values, half_values, 2
    )
    other_velocity = from_partner(sent_velocity, "cfg", 0)
    cond_first = half_index == 0
    conditional = jnp.where(cond_first, kept_velocity, other_velocity)
    unconditional = jnp.where(cond_first, other_velocity, kept_velocity)
    guided = unconditional + GUIDANCE * (conditional - unconditional)
    step_size = lax.dynamic_slice_in_dim(upcoming - current, offset, group_size, 0)
    next_latent = latent + step_size[:, None, None] * guided
    squares = jnp.sum(next_latent * next_latent, axis=(1, 2))
    largest = jnp.max(jnp.abs(next_latent), axis=(1, 2))
    square_total = lax.psum(squares, ("cfg", "seq"))
    peak_value = lax.pmax(largest, ("cfg", "seq"))
    latent_norm = jnp.sqrt(square_total / (IMG * PATCHC))
    return (guided, next_latent, latent_norm, peak_value)


def solution(mesh):
    placed = (
        P("cfg", "req", "seq", None),
        P("cfg", "req", "seq", None),
        P("cfg", None),
        P("cfg", None, None),
        P(),
        P("req", "seq", "cfg"),
        P(None, ("req", "seq")),
        P(("req", "seq")),
        P(None, None, "req"),
        P(None, None, "req"),
        P("req", None),
        P(None, "seq"),
        P("seq", None),
        P(),
    )
    return jax.shard_map(
        on_device,
        mesh=mesh,
        in_specs=placed,
        out_specs=(P("req", "seq", "cfg"), P("req", "seq", "cfg"), P("req"), P("req")),
        check_vma=False,
    )
```

profile of v0, /device:TPU:1, one launch (start us, length us, event | category | flops | bytes accessed | tf_op | source)
XLA Modules:
  0.0 808.6 jit_solution(5461950614559532431)
XLA Ops:
  9.5 299.6 %all-gather = f32[128,120,16]{1,2,0:T(8,128)S(1)} all-gather(f32[1,120,16]{1,2,0:T(8,128)S(1)} %fusion.18), channel_id=1, replica_groups=mesh['cfg'=2,'req'=8,'seq'=16] {'req','seq'}, dimensions={0}, use_global_device_ids=true | all-gather | bytes 990720 | tf_op jit(solution)/shard_map/all_gather | solution.py:91
  314.5 19.9 %all_gather.14 = bf16[16,10,1536]{2,1,0:T(8,128)(2,1)S(1)} all-gather(bf16[2,10,1536]{2,1,0:T(8,128)(2,1)S(1)} %fusion.42), channel_id=1, replica_groups=mesh['cfg'=2,'req'=8,'seq'=16] {'req'}, dimensions={0}, use_global_device_ids=true | all-gather | bytes 552960 | tf_op jit(solution)/shard_map/all_gather | solution.py:107
  334.4 13.0 %all_to_all.30 = bf16[16,10,1536]{2,1,0:T(8,128)(2,1)S(1)} all-to-all(bf16[16,10,1536]{2,1,0:T(8,128)(2,1)S(1)} %all_gather.14), channel_id=1, replica_groups=mesh['cfg'=2,'req'=8,'seq'=16] {'seq'}, dimensions={0} | all-to-all | bytes 983040 | tf_op jit(solution)/shard_map/all_to_all | solution.py:115
  347.4 51.1 %all-gather.4.cloned.1.call-done = bf16[16,32,1536]{2,1,0:T(8,128)(2,1)} async-done(((bf16[2,32,1536]{2,1,0:T(8,128)(2,1)}), bf16[16,32,1536]{2,1,0:T(8,128)(2,1)}) %all-gather.4.cloned.1.call-update) | async-done | bytes 1572880 | tf_op jit(solution)/shard_map/all_gather | solution.py:106
  398.5 5.8 all-to-all-start
  406.0 1.7 convolution_convert_fusion.3
  407.8 13.1 %all-to-all-done = bf16[16,32,1536]{2,1,0:T(8,128)(2,1)} async-done(((bf16[16,32,1536]{2,1,0:T(8,128)(2,1)}), bf16[16,32,1536]{2,1,0:T(8,128)(2,1)}, u32[]{:S(2)}, u32[]{:S(2)}) %all-to-all-start) | async-done | bytes 1572896 | tf_op jit(solution)/shard_map/all_to_all | solution.py:114
  420.9 2.5 convolution_convert_fusion.2
  423.5 3.5 fusion.63
  427.1 2.7 fusion.17
  430.4 4.1 copy.58
  435.0 11.5 %reduce.2 = bf16[512,1536]{1,0:T(8,128)(2,1)S(1)} reduce(bf16[512,1,1536]{2,1,0:T(2,128)(2,1)} %bitcast.126, bf16[]{:T(256)} %broadcast.203), dimensions={1}, to_apply=%bitcast.124.reduce_sub_computation | reduce | bytes 3145730
  446.5 2.1 reshape.184
  448.6 18.4 %all_to_all.31 = bf16[16,2,24576]{2,1,0:T(2,128)(2,1)S(1)} all-to-all(bf16[16,2,24576]{2,1,0:T(2,128)(2,1)} %reshape.184), channel_id=1, replica_groups=mesh['cfg'=2,'req'=8,'seq'=16] {'seq'}, dimensions={0} | all-to-all | bytes 3145728 | tf_op jit(solution)/shard_map/all_to_all | solution.py:153
  466.9 6.3 reshape.185
  473.2 3.4 copy.36
  477.3 42.2 %reduce-scatter.3.cloned.1.call-done = bf16[2,32,1536]{2,1,0:T(8,128)(2,1)} async-done(((bf16[16,32,1536]{2,1,0:T(8,128)(2,1)}), bf16[2,32,1536]{2,1,0:T(8,128)(2,1)}) %reduce-scatter.3.cloned.1.call-update) | async-done | bytes 196624 | tf_op jit(solution)/shard_map/reduce_scatter | solution.py:156
  521.7 1.8 add_convert_fusion.1
  523.5 54.8 %all-gather.6.cloned.1.call-done = bf16[2,512,1536]{2,1,0:T(8,128)(2,1)} async-done(((bf16[2,32,1536]{2,1,0:T(8,128)(2,1)}), bf16[2,512,1536]{2,1,0:T(8,128)(2,1)}) %all-gather.6.cloned.1.call-update) | async-done | bytes 3145744 | tf_op jit(solution)/shard_map/all_gather | solution.py:163
  578.4 7.6 convolution_convert_fusion
  586.6 78.8 %reduce-scatter.5.cloned.1.call-done = bf16[2,32,1536]{2,1,0:T(8,128)(2,1)} async-done(((bf16[2,512,1536]{2,1,0:T(8,128)(2,1)}), bf16[2,32,1536]{2,1,0:T(8,128)(2,1)}) %reduce-scatter.5.cloned.1.call-update) | async-done | bytes 196624 | tf_op jit(solution)/shard_map/reduce_scatter | solution.py:169
  669.1 2.4 collective-permute-start
  673.1 65.3 %psum.7 = f32[2]{0:T(128)S(1)} all-reduce(f32[2]{0:T(128)S(1)} %get-tuple-element.41), channel_id=1, replica_groups=mesh['cfg'=2,'req'=8,'seq'=16] {'cfg','seq'}, use_global_device_ids=true, to_apply=%region_13.14 | all-reduce | flops 2 | bytes 16 | tf_op jit(solution)/shard_map/psum | solution.py:192
  738.8 63.2 %pmax.7 = f32[2]{0:T(128)} all-reduce(f32[2]{0:T(128)S(1)} %get-tuple-element.40), channel_id=1, replica_groups=mesh['cfg'=2,'req'=8,'seq'=16] {'cfg','seq'}, use_global_device_ids=true, to_apply=%region_15.16 | all-reduce | flops 2 | bytes 16 | tf_op jit(solution)/shard_map/pmax | solution.py:193
  (85 shorter events, 19.9 us)
Async XLA Ops:
  7.2 413.7 %copy-start = (bf16[1536,3,192]{0,2,1:T(8,128)(2,1)S(1)}, bf16[1536,3,192]{0,2,1:T(8,128)(2,1)}, u32[]{:S(2)}) copy-start(bf16[1536,3,192]{0,2,1:T(8,128)(2,1)} %param.22) | copy-start | bytes 5308420
  7.2 391.3 %all-gather.4.cloned.1.call-start = ((), (), s32[]{:S(2)}) async-start(), calls=%async_computation.5 | async-start | bytes 1769472 | tf_op jit(solution)/shard_map/all_gather | solution.py:106
  309.4 3.5 copy-start.1
  309.4 4.7 copy-start.4
  347.4 57.1 %copy-start.13 = (s32[1,16]{1,0:T(1,128)S(1)}, s32[1,16]{1,0:T(1,128)}, u32[]{:S(2)}) copy-start(s32[1,16]{1,0:T(1,128)} %param.16) | copy-start | bytes 196
  398.5 22.4 %all-to-all-start = ((bf16[16,32,1536]{2,1,0:T(8,128)(2,1)}), bf16[16,32,1536]{2,1,0:T(8,128)(2,1)}, u32[]{:S(2)}, u32[]{:S(2)}) async-start(bf16[16,32,1536]{2,1,0:T(8,128)(2,1)} %all-gather.4.cloned.1.call-done), calls=%async_computation | async-start | bytes 3145728 | tf_op jit(solution)/shard_map/all_to_all | solution.py:114
  404.3 115.1 %reduce-scatter.3.cloned.1.call-start = ((), (), s32[]{:S(2)}) async-start(), calls=%async_computation.6 | async-start | bytes 1769472 | tf_op jit(solution)/shard_map/reduce_scatter | solution.py:156
  427.1 2.7 copy-start.3
  476.5 0.7 copy-start.5
  476.5 0.7 copy-start.8
  476.5 0.7 copy-start.9
  476.5 101.8 %copy-start.11 = (bf16[384,1536]{1,0:T(8,128)(2,1)S(1)}, bf16[384,1536]{1,0:T(8,128)(2,1)}, u32[]{:S(2)}) copy-start(bf16[384,1536]{1,0:T(8,128)(2,1)} %param.26) | copy-start | bytes 3538948
  476.6 101.8 %all-gather.6.cloned.1.call-start = ((), (), s32[]{:S(2)}) async-start(), calls=%async_computation.7 | async-start | bytes 3342336 | tf_op jit(solution)/shard_map/all_gather | solution.py:163
  523.5 142.0 %reduce-scatter.5.cloned.1.call-start = ((), (), s32[]{:S(2)}) async-start(), calls=%async_computation.8 | async-start | bytes 3342336 | tf_op jit(solution)/shard_map/reduce_scatter | solution.py:169
  585.9 0.7 copy-start.6
  585.9 0.7 copy-start.7
  585.9 79.6 %copy-start.2 = (bf16[2,32,1536]{2,1,0:T(8,128)(2,1)S(1)}, bf16[2,32,1536]{2,1,0:T(8,128)(2,1)}, u32[]{:S(2)}) copy-start(bf16[2,32,1536]{2,1,0:T(8,128)(2,1)} %reduce-scatter.3.cloned.1.call-done) | copy-start | bytes 589828
  585.9 81.9 %copy-start.12 = (bf16[1536,64]{0,1:T(8,128)(2,1)S(1)}, bf16[1536,64]{0,1:T(8,128)(2,1)}, u32[]{:S(2)}) copy-start(bf16[1536,64]{0,1:T(8,128)(2,1)} %param.27) | copy-start | bytes 589828
  585.9 86.4 %copy-start.10 = (f32[2,32,32]{2,1,0:T(8,128)S(1)}, f32[2,32,32]{2,1,0:T(8,128)}, u32[]{:S(2)}) copy-start(f32[2,32,32]{2,1,0:T(8,128)} %param.19) | copy-start | bytes 24580
  669.1 3.3 collective-permute-start
Sparse Core Ops, SparseCore 0:
  314.2 84.2 all-gather.3
  476.7 42.7 reduce-scatter.2
  523.6 54.7 all-gather.5
  586.1 79.3 reduce-scatter.4
where the time goes:
time: 809 us
  blocking collectives  479 us (59%)
  waiting for transfers between devices  241 us (30%)
  other arithmetic  23.5 us (3%)
  local copies, waits for them, and re-layouts  21.2 us (3%)
  matrix products  21.1 us (3%)
  between operations  14 us (2%)
  starting transfers between devices  8.55 us (1%)
    all_gather x1, blocking collectives, on_device(): every_mod = lax.all_gather(columns, ('req', 'seq'), axis=1, tiled=True)  300 us
    reduce_scatter x1, waiting for transfers between devices, on_device(): lax.psum_scatter(mlp_terms.astype(jnp.bfloat16), 'seq', scatter_dimension...  78.8 us
    psum x1, blocking collectives, on_device(): square_total = lax.psum(squares, ('cfg', 'seq'))  65.3 us
    pmax x1, blocking collectives, on_device(): peak_value = lax.pmax(largest, ('cfg', 'seq'))  63.2 us
    all_gather x1, waiting for transfers between devices, on_device(): lax.all_gather(mlp_in, 'seq', axis=1, tiled=True)  54.8 us
    all_gather x1, waiting for transfers between devices, on_device(): lax.all_gather(img_in, 'req', axis=0, tiled=True)  51.1 us
    reduce_scatter x1, waiting for transfers between devices, on_device(): lax.psum_scatter(moved_rows.astype(jnp.bfloat16), 'req', scatter_dimensio...  42.2 us
    all_gather x1, blocking collectives, on_device(): lax.all_gather(txt_in, 'req', axis=0, tiled=True)  19.9 us
  transfers between devices with their start and end apart: 6, of which 6 were waited for; matrix products, arithmetic and copies ran while one was open for 0% of the time, Pallas kernels for 0%

commit v1 on v0

--- a/solution.py
+++ b/solution.py
@@ -189,7 +189,7 @@
     next_latent = latent + step_size[:, None, None] * guided
     squares = jnp.sum(next_latent * next_latent, axis=(1, 2))
     largest = jnp.max(jnp.abs(next_latent), axis=(1, 2))
-    square_total = lax.psum(squares, ("cfg", "seq"))
+    square_total = jnp.sum(lax.all_gather(squares, ("cfg", "seq")), axis=0)
     peak_value = lax.pmax(largest, ("cfg", "seq"))
     latent_norm = jnp.sqrt(square_total / (IMG * PATCHC))
     return (guided, next_latent, latent_norm, peak_value)

time: 809 us -> 810 us (level)
    psum x1 -> x0, blocking collectives: 65.3 us -> none  [on_device(): square_total = lax.psum(squares, ('cfg', 'seq'))]
    unnamed x0 -> x1, blocking collectives: none -> 65 us
  transfers between devices with their start and end apart: 6 -> 6, of which waited for: 6 -> 5; matrix products, arithmetic and copies ran while one was open for 0% -> 1% of each run, Pallas kernels for 0% -> 0%
where the time goes in v1:
time: 810 us; the launch traced here: 809 us
  blocking collectives  479 us (59%)
  waiting for transfers between devices  240 us (30%)
  other arithmetic  23.6 us (3%)
  local copies, waits for them, and re-layouts  22 us (3%)
  matrix products  21.1 us (3%)
  between operations  14.7 us (2%)
  starting transfers between devices  8.55 us (1%)
    all_gather x1, blocking collectives, on_device(): every_mod = lax.all_gather(columns, ('req', 'seq'), axis=1, tiled=True)  300 us
    reduce_scatter x1, waiting for transfers between devices, on_device(): lax.psum_scatter(mlp_terms.astype(jnp.bfloat16), 'seq', scatter_dimension...  78.8 us
    unnamed x1, blocking collectives  65 us
    pmax x1, blocking collectives, on_device(): peak_value = lax.pmax(largest, ('cfg', 'seq'))  63.4 us
    all_gather x1, waiting for transfers between devices, on_device(): lax.all_gather(mlp_in, 'seq', axis=1, tiled=True)  54.8 us
    all_gather x1, waiting for transfers between devices, on_device(): lax.all_gather(img_in, 'req', axis=0, tiled=True)  51.1 us
    reduce_scatter x1, waiting for transfers between devices, on_device(): lax.psum_scatter(moved_rows.astype(jnp.bfloat16), 'req', scatter_dimensio...  42.2 us
    all_gather x1, blocking collectives, on_device(): lax.all_gather(txt_in, 'req', axis=0, tiled=True)  19.9 us
  transfers between devices with their start and end apart: 6, of which 5 were waited for; matrix products, arithmetic and copies ran while one was open for 1% of the time, Pallas kernels for 0%

profile of v1, /device:TPU:1, one launch (start us, length us, event | category | flops | bytes accessed | tf_op | source)
XLA Modules:
  0.0 809.3 jit_solution(5338575640614300922)
XLA Ops:
  9.5 299.6 %all-gather.1 = f32[128,120,16]{1,2,0:T(8,128)S(1)} all-gather(f32[1,120,16]{1,2,0:T(8,128)S(1)} %fusion.18), channel_id=1, replica_groups=mesh['cfg'=2,'req'=8,'seq'=16] {'req','seq'}, dimensions={0}, use_global_device_ids=true | all-gather | bytes 990720 | tf_op jit(solution)/shard_map/all_gather | solution.py:91
  314.5 19.9 %all_gather.20 = bf16[16,10,1536]{2,1,0:T(8,128)(2,1)S(1)} all-gather(bf16[2,10,1536]{2,1,0:T(8,128)(2,1)S(1)} %fusion.42), channel_id=1, replica_groups=mesh['cfg'=2,'req'=8,'seq'=16] {'req'}, dimensions={0}, use_global_device_ids=true | all-gather | bytes 552960 | tf_op jit(solution)/shard_map/all_gather | solution.py:107
  334.4 13.0 %all_to_all.30 = bf16[16,10,1536]{2,1,0:T(8,128)(2,1)S(1)} all-to-all(bf16[16,10,1536]{2,1,0:T(8,128)(2,1)S(1)} %all_gather.20), channel_id=1, replica_groups=mesh['cfg'=2,'req'=8,'seq'=16] {'seq'}, dimensions={0} | all-to-all | bytes 983040 | tf_op jit(solution)/shard_map/all_to_all | solution.py:115
  347.4 51.1 %all-gather.5.cloned.1.call-done = bf16[16,32,1536]{2,1,0:T(8,128)(2,1)} async-done(((bf16[2,32,1536]{2,1,0:T(8,128)(2,1)}), bf16[16,32,1536]{2,1,0:T(8,128)(2,1)}) %all-gather.5.cloned.1.call-update) | async-done | bytes 1572880 | tf_op jit(solution)/shard_map/all_gather | solution.py:106
  398.5 5.8 all-to-all-start
  406.0 1.7 convolution_convert_fusion.3
  407.8 13.1 %all-to-all-done = bf16[16,32,1536]{2,1,0:T(8,128)(2,1)} async-done(((bf16[16,32,1536]{2,1,0:T(8,128)(2,1)}), bf16[16,32,1536]{2,1,0:T(8,128)(2,1)}, u32[]{:S(2)}, u32[]{:S(2)}) %all-to-all-start) | async-done | bytes 1572896 | tf_op jit(solution)/shard_map/all_to_all | solution.py:114
  420.9 2.5 convolution_convert_fusion.2
  423.5 3.5 fusion.63
  427.1 2.7 fusion.17
  430.4 4.1 copy.58
  435.0 11.5 %reduce.2 = bf16[512,1536]{1,0:T(8,128)(2,1)S(1)} reduce(bf16[512,1,1536]{2,1,0:T(2,128)(2,1)} %bitcast.127, bf16[]{:T(256)} %broadcast.204), dimensions={1}, to_apply=%bitcast.125.reduce_sub_computation | reduce | bytes 3145730
  446.5 2.1 reshape.190
  448.6 18.4 %all_to_all.31 = bf16[16,2,24576]{2,1,0:T(2,128)(2,1)S(1)} all-to-all(bf16[16,2,24576]{2,1,0:T(2,128)(2,1)} %reshape.190), channel_id=1, replica_groups=mesh['cfg'=2,'req'=8,'seq'=16] {'seq'}, dimensions={0} | all-to-all | bytes 3145728 | tf_op jit(solution)/shard_map/all_to_all | solution.py:153
  466.9 6.3 reshape.191
  473.2 3.4 copy.36
  477.3 42.2 %reduce-scatter.3.cloned.1.call-done = bf16[2,32,1536]{2,1,0:T(8,128)(2,1)} async-done(((bf16[16,32,1536]{2,1,0:T(8,128)(2,1)}), bf16[2,32,1536]{2,1,0:T(8,128)(2,1)}) %reduce-scatter.3.cloned.1.call-update) | async-done | bytes 196624 | tf_op jit(solution)/shard_map/reduce_scatter | solution.py:156
  521.7 1.8 add_convert_fusion.1
  523.5 54.8 %all-gather.7.cloned.1.call-done = bf16[2,512,1536]{2,1,0:T(8,128)(2,1)} async-done(((bf16[2,32,1536]{2,1,0:T(8,128)(2,1)}), bf16[2,512,1536]{2,1,0:T(8,128)(2,1)}) %all-gather.7.cloned.1.call-update) | async-done | bytes 3145744 | tf_op jit(solution)/shard_map/all_gather | solution.py:163
  578.4 7.6 convolution_convert_fusion
  586.6 78.8 %reduce-scatter.5.cloned.1.call-done = bf16[2,32,1536]{2,1,0:T(8,128)(2,1)} async-done(((bf16[2,512,1536]{2,1,0:T(8,128)(2,1)}), bf16[2,32,1536]{2,1,0:T(8,128)(2,1)}) %reduce-scatter.5.cloned.1.call-update) | async-done | bytes 196624 | tf_op jit(solution)/shard_map/reduce_scatter | solution.py:169
  669.1 2.4 collective-permute-start
  673.7 65.0 %all-reduce = f32[64]{0:T(128)S(1)} all-reduce(f32[64]{0:T(128)S(1)} %dynamic-update-slice), channel_id=2, replica_groups=mesh['cfg'=2,'req'=8,'seq'=16] {'cfg','seq'}, use_global_device_ids=true, to_apply=%add | all-reduce | flops 64 | bytes 512
  739.4 63.4 %pmax.7 = f32[2]{0:T(128)} all-reduce(f32[2]{0:T(128)S(1)} %get-tuple-element.40), channel_id=1, replica_groups=mesh['cfg'=2,'req'=8,'seq'=16] {'cfg','seq'}, use_global_device_ids=true, to_apply=%region_15.16 | all-reduce | flops 2 | bytes 16 | tf_op jit(solution)/shard_map/pmax | solution.py:193
  (92 shorter events, 20.1 us)
Async XLA Ops:
  7.2 413.7 %copy-start = (bf16[1536,3,192]{0,2,1:T(8,128)(2,1)S(1)}, bf16[1536,3,192]{0,2,1:T(8,128)(2,1)}, u32[]{:S(2)}) copy-start(bf16[1536,3,192]{0,2,1:T(8,128)(2,1)} %param.22) | copy-start | bytes 5308420
  7.2 391.3 %all-gather.5.cloned.1.call-start = ((), (), s32[]{:S(2)}) async-start(), calls=%async_computation.5 | async-start | bytes 1769472 | tf_op jit(solution)/shard_map/all_gather | solution.py:106
  309.4 3.5 copy-start.1
  309.4 4.7 copy-start.4
  347.4 57.1 %copy-start.13 = (s32[1,16]{1,0:T(1,128)S(1)}, s32[1,16]{1,0:T(1,128)}, u32[]{:S(2)}) copy-start(s32[1,16]{1,0:T(1,128)} %param.16) | copy-start | bytes 196
  398.5 22.4 %all-to-all-start = ((bf16[16,32,1536]{2,1,0:T(8,128)(2,1)}), bf16[16,32,1536]{2,1,0:T(8,128)(2,1)}, u32[]{:S(2)}, u32[]{:S(2)}) async-start(bf16[16,32,1536]{2,1,0:T(8,128)(2,1)} %all-gather.5.cloned.1.call-done), calls=%async_computation | async-start | bytes 3145728 | tf_op jit(solution)/shard_map/all_to_all | solution.py:114
  404.3 115.1 %reduce-scatter.3.cloned.1.call-start = ((), (), s32[]{:S(2)}) async-start(), calls=%async_computation.6 | async-start | bytes 1769472 | tf_op jit(solution)/shard_map/reduce_scatter | solution.py:156
  427.1 2.7 copy-start.3
  476.5 0.7 copy-start.5
  476.5 0.7 copy-start.8
  476.5 0.7 copy-start.9
  476.5 101.8 %copy-start.11 = (bf16[384,1536]{1,0:T(8,128)(2,1)S(1)}, bf16[384,1536]{1,0:T(8,128)(2,1)}, u32[]{:S(2)}) copy-start(bf16[384,1536]{1,0:T(8,128)(2,1)} %param.26) | copy-start | bytes 3538948
  476.6 101.8 %all-gather.7.cloned.1.call-start = ((), (), s32[]{:S(2)}) async-start(), calls=%async_computation.7 | async-start | bytes 3342336 | tf_op jit(solution)/shard_map/all_gather | solution.py:163
  523.5 142.0 %reduce-scatter.5.cloned.1.call-start = ((), (), s32[]{:S(2)}) async-start(), calls=%async_computation.8 | async-start | bytes 3342336 | tf_op jit(solution)/shard_map/reduce_scatter | solution.py:169
  585.9 0.7 copy-start.6
  585.9 0.7 copy-start.7
  585.9 79.6 %copy-start.2 = (bf16[2,32,1536]{2,1,0:T(8,128)(2,1)S(1)}, bf16[2,32,1536]{2,1,0:T(8,128)(2,1)}, u32[]{:S(2)}) copy-start(bf16[2,32,1536]{2,1,0:T(8,128)(2,1)} %reduce-scatter.3.cloned.1.call-done) | copy-start | bytes 589828
  585.9 81.9 %copy-start.12 = (bf16[1536,64]{0,1:T(8,128)(2,1)S(1)}, bf16[1536,64]{0,1:T(8,128)(2,1)}, u32[]{:S(2)}) copy-start(bf16[1536,64]{0,1:T(8,128)(2,1)} %param.27) | copy-start | bytes 589828
  585.9 85.6 %copy-start.14 = (u32[256]{0:T(256)S(1)}, u32[256]{0:T(256)}, u32[]{:S(2)}) copy-start(u32[256]{0:T(256)} %constant.136) | copy-start | bytes 3076
  586.0 86.8 %copy-start.10 = (f32[2,32,32]{2,1,0:T(8,128)S(1)}, f32[2,32,32]{2,1,0:T(8,128)}, u32[]{:S(2)}) copy-start(f32[2,32,32]{2,1,0:T(8,128)} %param.19) | copy-start | bytes 24580
  669.1 3.7 collective-permute-start
Sparse Core Ops, SparseCore 0:
  314.2 84.2 all-gather.4
  476.7 42.7 reduce-scatter.2
  523.6 54.7 all-gather.6
  586.1 79.3 reduce-scatter.4
